TPU v7x, 256 devices: a whole 4x4x8 slice. The times are simulated.
256 devices in a mesh: act: 32 (over x, y, core), pix: 8 (over z).
Axes of the slice: x: 4, y: 4, z: 8, core: 2. Of those that a mesh axis runs over, the one named last changes fastest.
Arguments:
- pixel_index: int32 [8, 512], P('pix'), may hold values from 0 to 65535
- act_map: int32 [32768], P('act'), may hold values from 0 to 32767, each once
- omega: bfloat16 [32768, 128], P('act'), may hold values from -6 to 6
- pupil_field: float32 [8, 2, 32768], P('pix', None, 'act'), may hold values from -6 to 6
- channel_scale: float32 [8], P('pix'), may hold values from 0.9 to 1.1
- channel_flux: float32 [8], P('pix'), may hold values from 0.3 to 3
Outputs:
- basis_out: float32 [8, 1024, 128], P('pix', 'act')
- projection: float32 [128, 32768], P('pix', 'act')
- r_factor: float32 [128, 128], replicated
Inputs may be any that keep to these rules, and one draw needn't show every extreme that they name: `act_map`: every number of 0 to 32767 appears once. `pixel_index`: pixels of a channel may repeat.
All inputs are finite; a program needn't handle non-finite values.
Results may differ from a plain program's by a relative error of at most 0.0048.
Values may be sent and summed in bfloat16 or wider, within the bound.
No kernel may reach another device: no remote copies, remote signals or barrier semaphores. Data moves between devices by JAX's collectives and lax.ppermute only.
A program may use at most 64 MiB of HBM per device.

v0:
```python
import math
import jax
import jax.numpy as jnp
from jax import lax
from jax.sharding import PartitionSpec as P

GRID = 128
FOCAL = 256
RANK = 128
ACT = 32768
TWO_PI = 2.0 * math.pi
INFL_RATE = 4.5
DEFOCUS_RATE = 6.0


def jacobian_planes(pixels, wave_scale, flux_level, codes, field_re, field_im):
    delta_u = pixels // FOCAL - FOCAL // 2
    delta_v = pixels % FOCAL - FOCAL // 2
    mirror = codes // (GRID * GRID)
    column_x = codes // GRID % GRID - GRID // 2
    column_y = codes % GRID - GRID // 2
    phase_int = delta_u[:, None] * column_x[None, :] + delta_v[:, None] * column_y[None, :]
    radius = (delta_u * delta_u + delta_v * delta_v).astype(jnp.float32)
    amplitude = flux_level * jnp.exp(-INFL_RATE * radius / (FOCAL * FOCAL))
    defocus = radius * (TWO_PI * DEFOCUS_RATE / (FOCAL * FOCAL)) / wave_scale
    phase_angle = mirror.astype(jnp.float32)[None, :] * defocus[
        :, None
    ] - TWO_PI / FOCAL * wave_scale * phase_int.astype(jnp.float32)
    cosine = jnp.cos(phase_angle)
    sine_part = jnp.sin(phase_angle)
    real_part = amplitude[:, None] * (field_re[None, :] * cosine - field_im[None, :] * sine_part)
    imag_part = amplitude[:, None] * (field_re[None, :] * sine_part + field_im[None, :] * cosine)
    return (real_part.astype(jnp.bfloat16), imag_part.astype(jnp.bfloat16))


def gram_of(sketch):
    return lax.dot_general(
        sketch,
        sketch,
        (((0,), (0,)), ((), ())),
        precision=lax.Precision.HIGHEST,
        preferred_element_type=jnp.float32,
    )


def on_device(pixel_index, act_map, omega, pupil_field, channel_scale, channel_flux):
    pixels = pixel_index[0]
    npix = pixels.shape[0]
    rows_dev = 2 * npix
    act_count = lax.axis_size("act")
    pix_count = lax.axis_size("pix")
    total_rows = rows_dev * pix_count
    share_pix = npix // act_count
    real_rows, imag_rows = jacobian_planes(
        pixels, channel_scale[0], channel_flux[0], act_map, pupil_field[0, 0], pupil_field[0, 1]
    )
    jac = jnp.concatenate([real_rows, imag_rows], axis=0)
    partial_sketch = jnp.dot(jac, omega, preferred_element_type=jnp.float32)
    sketch = lax.psum(partial_sketch, "act")
    gram_matrix = lax.psum(gram_of(sketch), "pix")
    lower_factor = jnp.linalg.cholesky(gram_matrix)
    basis = jax.scipy.linalg.solve_triangular(lower_factor, sketch.T, lower=True).T
    first = lax.axis_index("act") * share_pix
    own_re = lax.dynamic_slice_in_dim(basis, first, share_pix, 0)
    own_im = lax.dynamic_slice_in_dim(basis, npix + first, share_pix, 0)
    own_basis = jnp.stack([own_re, own_im], axis=1).reshape(2 * share_pix, RANK)
    coarse = basis.astype(jnp.bfloat16)
    partial_value = lax.dot_general(
        coarse, jac, (((0,), (0,)), ((), ())), preferred_element_type=jnp.float32
    )
    projection = lax.psum_scatter(partial_value, "pix", scatter_dimension=0, tiled=True)
    basis_out = (own_basis * math.sqrt(total_rows)).reshape(1, 2 * share_pix, RANK)
    r_factor = lower_factor.T / math.sqrt(total_rows * ACT)
    return (basis_out, projection, r_factor)


def solution(mesh):
    return jax.shard_map(
        on_device,
        mesh=mesh,
        in_specs=(
            P("pix", None),
            P("act"),
            P("act", None),
            P("pix", None, "act"),
            P("pix"),
            P("pix"),
        ),
        out_specs=(P("pix", "act", None), P("pix", "act"), P()),
        check_vma=False,
    )
```

profile of v0, /device:TPU:2, one launch (start us, length us, event | category | flops | bytes accessed | tf_op | source)
XLA Modules:
  0.0 285.0 jit_solution(6364925790602597482)
XLA Ops:
  7.2 0.0 copy-start
  7.2 0.0 all-reduce.3.cloned.1.call-start
  7.9 0.7 fusion.16
  8.6 0.7 exponential_multiply_fusion
  10.0 0.7 fusion.9
  10.7 0.8 fusion.21
  11.4 0.7 multiply_divide_fusion
  12.1 9.1 %multiply_convert_fusion.1 = (bf16[512,1024]{1,0:T(8,128)(2,1)S(1)}, bf16[512,1024]{1,0:T(8,128)(2,1)S(1)}) fusion(f32[1024]{0:T(1024)S(1)} %bitcast.32, s32[1024]{0:T(1024)S(1)} %get-tuple-element.17, s32[512]{0:T(512)S(1)} %fusion.16, s32[1024]{0:T(1024)S(1)} %get-tuple-element.18, s32[512]{0:T(512)S(1)} %get-tuple-element.7, f32[]{:T(128)S(6)} %mul_shard_map.3, ...), kind=kLoop, calls=%fused_computation.2 | loop fusion | flops 8912896 | bytes 2125828 | tf_op jit(solution)/shard_map/convert_element_type | solution.py:33
  21.2 0.0 copy-done
  21.2 1.5 fusion.3
  22.7 0.0 all-reduce.3.cloned.1.call-update
  22.8 0.0 all-reduce.5.cloned.1.call-start
  22.8 116.9 %all-reduce.3.cloned.1.call-done = f32[1024,128]{1,0:T(8,128)} async-done(((f32[1024,128]{1,0:T(8,128)}), f32[1024,128]{1,0:T(8,128)}) %all-reduce.3.cloned.1.call-update) | async-done | bytes 524304 | tf_op jit(solution)/shard_map/psum | solution.py:59
  139.7 0.0 copy-start.1
  139.7 2.9 %fusion.22 = f32[128,128]{0,1:T(8,128)} fusion(f32[1024,128]{1,0:T(8,128)} %all-reduce.3.cloned.1.call-done), kind=kOutput, calls=%fused_computation.58 | convolution fusion | flops 201326592 | bytes 589824 | tf_op jit(solution)/shard_map/dot_general | solution.py:37
  142.6 0.0 all-reduce.5.cloned.1.call-update
  142.7 0.0 reduce-scatter.2.cloned.1.call-start
  142.7 72.8 %all-reduce.5.cloned.1.call-done = f32[128,128]{0,1:T(8,128)} async-done(((f32[128,128]{0,1:T(8,128)}), f32[128,128]{0,1:T(8,128)}) %all-reduce.5.cloned.1.call-update) | async-done | bytes 65552 | tf_op jit(solution)/shard_map/psum | solution.py:60
  215.5 0.9 copy.10
  216.4 0.9 fusion.7
  217.3 11.7 %cholesky.16 = f32[128,128]{1,0:T(8,128)S(1)} custom-call(f32[128,128]{1,0:T(8,128)S(1)} %fusion.7), custom_call_target="Cholesky" | custom-call | tf_op jit(solution)/shard_map/jit(cholesky)/cholesky | solution.py:61
  229.0 0.6 compare_reduce_fusion
  229.7 0.7 multiply_bitcast_fusion
  230.3 9.8 %custom-call.7 = f32[1,128,128]{1,2,0:T(8,128)S(1)} custom-call(f32[1,128,128]{2,1,0:T(8,128)S(1)} %get-tuple-element.11), custom_call_target="InvertDiagBlocksLowerTriangular" | custom-call | tf_op jit(solution)/shard_map/jit(_solve_triangular)/triangular_solve | solution.py:62
  240.1 0.0 copy-done.1
  240.1 0.6 fusion.5
  240.7 1.3 fusion.2
  242.0 0.0 reduce-scatter.2.cloned.1.call-update
  242.0 0.7 copy.11
  242.7 0.6 maximum_multiply_fusion
  243.4 35.1 %reduce-scatter.2.cloned.1.call-done = f32[16,1024]{1,0:T(8,128)} async-done(((f32[128,1024]{1,0:T(8,128)}), f32[16,1024]{1,0:T(8,128)}) %reduce-scatter.2.cloned.1.call-update) | async-done | bytes 65552 | tf_op jit(solution)/shard_map/reduce_scatter | solution.py:71
  (2 shorter events, 0.0 us)
Async XLA Ops:
  7.2 14.1 %copy-start = (bf16[1024,128]{1,0:T(8,128)(2,1)S(1)}, bf16[1024,128]{1,0:T(8,128)(2,1)}, u32[]{:S(2)}) copy-start(bf16[1024,128]{1,0:T(8,128)(2,1)} %param.8) | copy-start | bytes 786436
  7.2 132.6 %all-reduce.3.cloned.1.call-start = ((), (), s32[]{:S(2)}) async-start(), calls=%async_computation.1 | async-start | bytes 1048576 | tf_op jit(solution)/shard_map/psum | solution.py:59
  22.8 192.7 %all-reduce.5.cloned.1.call-start = ((), (), s32[]{:S(2)}) async-start(), calls=%async_computation.2 | async-start | bytes 131072 | tf_op jit(solution)/shard_map/psum | solution.py:60
  139.7 100.4 %copy-start.1 = (f32[1024,128]{1,0:T(8,128)S(1)}, f32[1024,128]{1,0:T(8,128)}, u32[]{:S(2)}) copy-start(f32[1024,128]{1,0:T(8,128)} %all-reduce.3.cloned.1.call-done) | copy-start | bytes 1572868
  142.7 135.8 %reduce-scatter.2.cloned.1.call-start = ((), (), s32[]{:S(2)}) async-start(), calls=%async_computation.3 | async-start | bytes 589824 | tf_op jit(solution)/shard_map/reduce_scatter | solution.py:71
Sparse Core Ops, SparseCore 0:
  22.9 116.8 all-reduce.2
  142.8 72.6 all-reduce.4
  242.1 36.2 reduce-scatter.1
where the time goes:
time: 285 us
  waiting for transfers between devices  225 us (79%)
  other arithmetic  36.2 us (13%)
  between operations  15.2 us (5%)
  matrix products  6.22 us (2%)
    psum x1, waiting for transfers between devices, on_device(): sketch = lax.psum(partial_sketch, 'act')  117 us
    psum x1, waiting for transfers between devices, on_device(): gram_matrix = lax.psum(gram_of(sketch), 'pix')  72.8 us
    reduce_scatter x1, waiting for transfers between devices, on_device(): lax.psum_scatter(partial_value, 'pix', scatter_dimension=0, tiled=True)  35.1 us
    another operation x3, other arithmetic, on_device(): lower_factor = jnp.linalg.cholesky(gram_matrix)  12.4 us
    another operation x1, other arithmetic, on_device(): jax.scipy.linalg.solve_triangular(lower_factor, sketch.T, lower=True)  9.81 us
    convert_element_type x1, other arithmetic, jacobian_planes(): return (real_part.astype(jnp.bfloat16), imag_part.astype(jnp.bfloat16))  9.06 us
  transfers between devices with their start and end apart: 3, of which 3 were waited for; matrix products, arithmetic and copies ran while one was open for 0% of the time, Pallas kernels for 0%

commit v1 on v0

--- a/solution.py
+++ b/solution.py
@@ -56,7 +56,18 @@
     )
     jac = jnp.concatenate([real_rows, imag_rows], axis=0)
     partial_sketch = jnp.dot(jac, omega, preferred_element_type=jnp.float32)
-    sketch = lax.psum(partial_sketch, "act")
+
+    def _begin_object(xin):
+        peer_axis = "act"
+        n_now = xin
+        extent = jax.lax.axis_size(peer_axis)
+        for it in [rr for rr in (1, 2, 4, 8, 16) if rr < extent]:
+            n_now = n_now + jax.lax.ppermute(
+                n_now, peer_axis, list(map(lambda at: (at, at ^ it), range(extent)))
+            )
+        return n_now
+
+    sketch = _begin_object(partial_sketch)
     gram_matrix = lax.psum(gram_of(sketch), "pix")
     lower_factor = jnp.linalg.cholesky(gram_matrix)
     basis = jax.scipy.linalg.solve_triangular(lower_factor, sketch.T, lower=True).T

time: 285 us -> 226 us (0.79)
  waiting for transfers between devices: 225 us -> 157 us
  starting transfers between devices: 0.12 us -> 9.34 us
    psum x1 -> x0, waiting for transfers between devices: 117 us -> none  [on_device(): sketch = lax.psum(partial_sketch, 'act')]
    ppermute x0 -> x5, waiting for transfers between devices: none -> 47.8 us  [_begin_object(): jax.lax.ppermute(n_now, peer_axis, list(map(lambda at: (at, at ^ it), ran...]
    ppermute x0 -> x5, starting transfers between devices: none -> 9.08 us  [_begin_object(): jax.lax.ppermute(n_now, peer_axis, list(map(lambda at: (at, at ^ it), ran...]
  transfers between devices with their start and end apart: 3 -> 7, of which waited for: 3 -> 7; matrix products, arithmetic and copies ran while one was open for 0% -> 1% of each run, Pallas kernels for 0% -> 0%
where the time goes in v1:
time: 226 us; the launch traced here: 225 us
  waiting for transfers between devices  157 us (69%)
  other arithmetic  36.5 us (16%)
  between operations  15.5 us (7%)
  starting transfers between devices  9.34 us (4%)
  matrix products  4.17 us (2%)
  local copies, waits for them, and re-layouts  2.45 us (1%)
    psum x1, waiting for transfers between devices, on_device(): gram_matrix = lax.psum(gram_of(sketch), 'pix')  74.4 us
    ppermute x5, waiting for transfers between devices, _begin_object(): jax.lax.ppermute(n_now, peer_axis, list(map(lambda at: (at, at ^ it), ran...  47.8 us
    reduce_scatter x1, waiting for transfers between devices, on_device(): lax.psum_scatter(partial_value, 'pix', scatter_dimension=0, tiled=True)  35 us
    another operation x3, other arithmetic, on_device(): lower_factor = jnp.linalg.cholesky(gram_matrix)  12.4 us
    another operation x1, other arithmetic, on_device(): jax.scipy.linalg.solve_triangular(lower_factor, sketch.T, lower=True)  9.81 us
    ppermute x5, starting transfers between devices, _begin_object(): jax.lax.ppermute(n_now, peer_axis, list(map(lambda at: (at, at ^ it), ran...  9.08 us
    convert_element_type x1, other arithmetic, jacobian_planes(): return (real_part.astype(jnp.bfloat16), imag_part.astype(jnp.bfloat16))  9.06 us
  transfers between devices with their start and end apart: 7, of which 7 were waited for; matrix products, arithmetic and copies ran while one was open for 1% of the time, Pallas kernels for 0%

profile of v1, /device:TPU:2, one launch (start us, length us, event | category | flops | bytes accessed | tf_op | source)
XLA Modules:
  0.0 225.2 jit_solution(9387717641315229778)
XLA Ops:
  7.2 0.0 copy-start
  7.2 0.0 all-reduce.2.cloned.1.call-start
  7.9 0.7 fusion.16
  8.6 0.7 exponential_multiply_fusion
  10.0 0.7 fusion.9
  10.7 0.8 fusion.21
  11.4 0.7 multiply_divide_fusion
  12.1 9.1 %multiply_convert_fusion.1 = (bf16[512,1024]{1,0:T(8,128)(2,1)S(1)}, bf16[512,1024]{1,0:T(8,128)(2,1)S(1)}) fusion(f32[1024]{0:T(1024)S(1)} %bitcast.32, s32[1024]{0:T(1024)S(1)} %get-tuple-element.17, s32[512]{0:T(512)S(1)} %fusion.16, s32[1024]{0:T(1024)S(1)} %get-tuple-element.18, s32[512]{0:T(512)S(1)} %get-tuple-element.7, f32[]{:T(128)S(6)} %mul_shard_map.3, ...), kind=kLoop, calls=%fused_computation.2 | loop fusion | flops 8912896 | bytes 2125828 | tf_op jit(solution)/shard_map/convert_element_type | solution.py:33
  21.2 0.0 copy-done
  21.2 0.7 fusion.3
  21.9 0.1 collective-permute-start
  22.0 1.9 collective-permute-done
  23.9 0.1 add.124
  24.0 1.7 collective-permute-start.1
  25.7 12.4 %collective-permute-done.1 = f32[1024,128]{1,0:T(8,128)S(1)} collective-permute-done((f32[1024,128]{1,0:T(8,128)S(1)}, f32[1024,128]{1,0:T(8,128)S(1)}, u32[]{:S(2)}, u32[]{:S(2)}) %collective-permute-start.1) | collective-permute-done | bytes 524320 | tf_op jit(solution)/shard_map/ppermute | solution.py:65
  38.1 0.1 add.125
  38.1 3.3 %collective-permute-start.2 = (f32[1024,128]{1,0:T(8,128)S(1)}, f32[1024,128]{1,0:T(8,128)S(1)}, u32[]{:S(2)}, u32[]{:S(2)}) collective-permute-start(f32[1024,128]{1,0:T(8,128)S(1)} %add.125), channel_id=1, source_target_pairs={{0,32},{8,40},{16,48},{24,56},{32,0},{40,8},{48,16},{56,24},{64,96... | collective-permute-start | bytes 1572872 | tf_op jit(solution)/shard_map/ppermute | solution.py:65
  41.4 11.4 %collective-permute-done.2 = f32[1024,128]{1,0:T(8,128)S(1)} collective-permute-done((f32[1024,128]{1,0:T(8,128)S(1)}, f32[1024,128]{1,0:T(8,128)S(1)}, u32[]{:S(2)}, u32[]{:S(2)}) %collective-permute-start.2) | collective-permute-done | bytes 524320 | tf_op jit(solution)/shard_map/ppermute | solution.py:65
  52.8 0.1 add.126
  52.9 2.3 %collective-permute-start.3 = (f32[1024,128]{1,0:T(8,128)S(1)}, f32[1024,128]{1,0:T(8,128)S(1)}, u32[]{:S(2)}, u32[]{:S(2)}) collective-permute-start(f32[1024,128]{1,0:T(8,128)S(1)} %add.126), channel_id=1, source_target_pairs={{0,64},{8,72},{16,80},{24,88},{32,96},{40,104},{48,112},{56,120},{... | collective-permute-start | bytes 1572872 | tf_op jit(solution)/shard_map/ppermute | solution.py:65
  55.2 10.5 %collective-permute-done.3 = f32[1024,128]{1,0:T(8,128)S(1)} collective-permute-done((f32[1024,128]{1,0:T(8,128)S(1)}, f32[1024,128]{1,0:T(8,128)S(1)}, u32[]{:S(2)}, u32[]{:S(2)}) %collective-permute-start.3) | collective-permute-done | bytes 524320 | tf_op jit(solution)/shard_map/ppermute | solution.py:65
  65.7 0.1 add.127
  65.8 1.7 collective-permute-start.4
  67.5 11.6 %collective-permute-done.4 = f32[1024,128]{1,0:T(8,128)S(1)} collective-permute-done((f32[1024,128]{1,0:T(8,128)S(1)}, f32[1024,128]{1,0:T(8,128)S(1)}, u32[]{:S(2)}, u32[]{:S(2)}) %collective-permute-start.4) | collective-permute-done | bytes 524320 | tf_op jit(solution)/shard_map/ppermute | solution.py:65
  79.1 0.1 add.128
  79.1 1.6 fusion.22
  80.8 0.0 all-reduce.2.cloned.1.call-update
  80.8 0.2 reduce-scatter.2.cloned.1.call-start
  81.0 74.4 %all-reduce.2.cloned.1.call-done = f32[128,128]{0,1:T(8,128)} async-done(((f32[128,128]{0,1:T(8,128)}), f32[128,128]{0,1:T(8,128)}) %all-reduce.2.cloned.1.call-update) | async-done | bytes 65552 | tf_op jit(solution)/shard_map/psum | solution.py:71
  155.4 0.9 copy.10
  156.4 0.9 fusion.7
  157.2 11.7 %cholesky.16 = f32[128,128]{1,0:T(8,128)S(1)} custom-call(f32[128,128]{1,0:T(8,128)S(1)} %fusion.7), custom_call_target="Cholesky" | custom-call | tf_op jit(solution)/shard_map/jit(cholesky)/cholesky | solution.py:72
  169.0 0.6 compare_reduce_fusion
  169.6 0.7 multiply_bitcast_fusion
  170.3 9.8 %custom-call.7 = f32[1,128,128]{1,2,0:T(8,128)S(1)} custom-call(f32[1,128,128]{2,1,0:T(8,128)S(1)} %get-tuple-element.11), custom_call_target="InvertDiagBlocksLowerTriangular" | custom-call | tf_op jit(solution)/shard_map/jit(_solve_triangular)/triangular_solve | solution.py:73
  180.1 0.6 fusion.5
  180.7 1.3 fusion.2
  182.0 0.0 reduce-scatter.2.cloned.1.call-update
  182.0 0.7 copy.11
  182.7 0.6 maximum_multiply_fusion
  183.3 35.0 %reduce-scatter.2.cloned.1.call-done = f32[16,1024]{1,0:T(8,128)} async-done(((f32[128,1024]{1,0:T(8,128)}), f32[16,1024]{1,0:T(8,128)}) %reduce-scatter.2.cloned.1.call-update) | async-done | bytes 65552 | tf_op jit(solution)/shard_map/reduce_scatter | solution.py:82
  (2 shorter events, 0.0 us)
Async XLA Ops:
  7.2 14.1 %copy-start = (bf16[1024,128]{1,0:T(8,128)(2,1)S(1)}, bf16[1024,128]{1,0:T(8,128)(2,1)}, u32[]{:S(2)}) copy-start(bf16[1024,128]{1,0:T(8,128)(2,1)} %param.8) | copy-start | bytes 786436
  7.2 148.3 %all-reduce.2.cloned.1.call-start = ((), (), s32[]{:S(2)}) async-start(), calls=%async_computation.1 | async-start | bytes 131072 | tf_op jit(solution)/shard_map/psum | solution.py:71
  21.9 2.0 collective-permute-start
  24.0 14.1 %collective-permute-start.1 = (f32[1024,128]{1,0:T(8,128)S(1)}, f32[1024,128]{1,0:T(8,128)S(1)}, u32[]{:S(2)}, u32[]{:S(2)}) collective-permute-start(f32[1024,128]{1,0:T(8,128)S(1)} %add.124), channel_id=1, source_target_pairs={{0,16},{8,24},{16,0},{24,8},{32,48},{40,56},{48,32},{56,40},{64,80... | collective-permute-start | bytes 1572872 | tf_op jit(solution)/shard_map/ppermute | solution.py:65
  38.1 14.7 %collective-permute-start.2 = (f32[1024,128]{1,0:T(8,128)S(1)}, f32[1024,128]{1,0:T(8,128)S(1)}, u32[]{:S(2)}, u32[]{:S(2)}) collective-permute-start(f32[1024,128]{1,0:T(8,128)S(1)} %add.125), channel_id=1, source_target_pairs={{0,32},{8,40},{16,48},{24,56},{32,0},{40,8},{48,16},{56,24},{64,96... | collective-permute-start | bytes 1572872 | tf_op jit(solution)/shard_map/ppermute | solution.py:65
  52.9 12.8 %collective-permute-start.3 = (f32[1024,128]{1,0:T(8,128)S(1)}, f32[1024,128]{1,0:T(8,128)S(1)}, u32[]{:S(2)}, u32[]{:S(2)}) collective-permute-start(f32[1024,128]{1,0:T(8,128)S(1)} %add.126), channel_id=1, source_target_pairs={{0,64},{8,72},{16,80},{24,88},{32,96},{40,104},{48,112},{56,120},{... | collective-permute-start | bytes 1572872 | tf_op jit(solution)/shard_map/ppermute | solution.py:65
  65.8 13.3 %collective-permute-start.4 = (f32[1024,128]{1,0:T(8,128)S(1)}, f32[1024,128]{1,0:T(8,128)S(1)}, u32[]{:S(2)}, u32[]{:S(2)}) collective-permute-start(f32[1024,128]{1,0:T(8,128)S(1)} %add.127), channel_id=1, source_target_pairs={{0,128},{8,136},{16,144},{24,152},{32,160},{40,168},{48,176},{56,1... | collective-permute-start | bytes 1572872 | tf_op jit(solution)/shard_map/ppermute | solution.py:65
  80.8 137.6 %reduce-scatter.2.cloned.1.call-start = ((), (), s32[]{:S(2)}) async-start(), calls=%async_computation.2 | async-start | bytes 589824 | tf_op jit(solution)/shard_map/reduce_scatter | solution.py:82
Sparse Core Ops, SparseCore 0:
  80.9 74.4 all-reduce.1
  182.1 36.2 reduce-scatter.1
